TPU v7x, 512 devices: a whole 4x4x16 slice. The times are simulated.
512 devices in a mesh: acq: 16 (over y_lo, x, core), pulse: 32 (over y_hi, z).
Axes of the slice: x: 4, y: 4 (y_hi: 2, y_lo: 2; y = y_hi * 2 + y_lo), z: 16, core: 2. Of those that a mesh axis runs over, the one named last changes fastest.
Arguments:
- raw_echo: bfloat16 [16, 2, 8192, 1535], P('acq', None, 'pulse'), may hold values from -6 to 6
- chirp_phase: float32 [1024], replicated, may hold values from -3.140625 to 3.140625
- pulse_counts: int32 [16], P('acq'), may hold values from 4096 to 8192, as said below
- azimuth_rate: float32 [512], P('pulse'), may hold values from 0.25 to 1
- partner_bits: int32 [16, 2], P('acq'), may hold values from 0 to 3, as said below
Outputs:
- interfere_real: float32 [16, 2, 128, 512], P('acq', None, 'pulse')
- interfere_imag: float32 [16, 2, 128, 512], P('acq', None, 'pulse')
Inputs may be any that keep to these rules, and one draw needn't show every extreme that they name: `pulse_counts`: at least half of 8192; some acquisition records all 8192 pulses and some exactly half. `partner_bits`: the two bits of a row differ.
All inputs are finite; a program needn't handle non-finite values.
Results may differ from a plain program's by a relative error of at most 0.0065.
Values may be sent and summed in bfloat16 or wider, within the bound.
No kernel may reach another device: no remote copies, remote signals or barrier semaphores. Data moves between devices by JAX's collectives and lax.ppermute only.
A program may use at most 64 MiB of HBM per device.

v0:
```python
import math
import jax
import jax.numpy as jnp
from jax import lax
from jax.sharding import PartitionSpec as P

RNG = 512
TAPS = 1024
LOOK_RNG = 4
LOOK_AZ = 16


def part_tables(length, inverse):
    steps = jnp.arange(length, dtype=jnp.int32)
    angle = 2.0 * jnp.pi * (steps[:, None] * steps[None, :] % length).astype(jnp.float32) / length
    cosine = jnp.cos(angle)
    sine = jnp.sin(angle)
    if inverse:
        sine = -sine
    return jnp.stack([jnp.stack([cosine, -sine]), jnp.stack([sine, cosine])])


def complex_product(left_re, left_im, right_re, right_im):
    return (left_re * right_re - left_im * right_im, left_re * right_im + left_im * right_re)


def compress(echoes, toeplitz, first_pulse, live_pulses, block_cols, window):
    pulse_rows = echoes.shape[1]
    parts_re = []
    parts_im = []
    for start in range(0, RNG, block_cols):
        segment = echoes[:, :, start : start + window]
        stacked = jnp.concatenate([segment[0], segment[1]], axis=1)
        result = lax.dot_general(
            toeplitz, stacked, (((1,), (1,)), ((), ())), preferred_element_type=jnp.float32
        )
        parts_re.append(result[:block_cols])
        parts_im.append(result[block_cols:])
    joined = jnp.stack([jnp.concatenate(parts_re, axis=0), jnp.concatenate(parts_im, axis=0)])
    pulse_ids = first_pulse + jnp.arange(pulse_rows, dtype=jnp.int32)
    keep = (pulse_ids < live_pulses).astype(jnp.float32)
    return (joined * keep[None, None, :]).astype(jnp.bfloat16)


def azimuth(turned, azimuth_rate):
    columns = turned.shape[1]
    length = turned.shape[2]
    outer_len = 64
    inner_len = length // outer_len
    highest = lax.Precision.HIGHEST
    signal = turned.astype(jnp.float32).reshape(2, columns, outer_len, inner_len)
    section_one = jnp.einsum(
        "pcab,pqak->qckb", signal, part_tables(outer_len, False), precision=highest
    )
    outer_ids = jnp.arange(outer_len, dtype=jnp.int32)
    inner_ids = jnp.arange(inner_len, dtype=jnp.int32)
    twist = (
        2.0
        * jnp.pi
        * (outer_ids[:, None] * inner_ids[None, :] % length).astype(jnp.float32)
        / length
    )
    twist_cos = jnp.cos(twist)
    twist_sin = jnp.sin(twist)
    turned_re, turned_im = complex_product(section_one[0], section_one[1], twist_cos, -twist_sin)
    spectrum = jnp.einsum(
        "pckb,pqbm->qckm",
        jnp.stack([turned_re, turned_im]),
        part_tables(inner_len, False),
        precision=highest,
    )
    freq_index = outer_ids[:, None] + outer_len * inner_ids[None, :]
    signed = jnp.where(freq_index < length // 2, freq_index, freq_index - length).astype(
        jnp.float32
    )
    quad = signed * signed / length
    phase = (jnp.pi * azimuth_rate)[:, None, None] * quad[None, :, :]
    filt_re, filt_im = complex_product(spectrum[0], spectrum[1], jnp.cos(phase), -jnp.sin(phase))
    back_one = jnp.einsum(
        "pckm,pqmb->qckb",
        jnp.stack([filt_re, filt_im]),
        part_tables(inner_len, True),
        precision=highest,
    )
    undo_re, undo_im = complex_product(back_one[0], back_one[1], twist_cos, twist_sin)
    restored = jnp.einsum(
        "pckb,pqka->qcab",
        jnp.stack([undo_re, undo_im]),
        part_tables(outer_len, True),
        precision=highest,
    )
    return (restored / length).reshape(2, columns, length)


def parity(index):
    return bin(index).count("1") % 2


def multilook(stacked):
    count, columns, pulse_len = stacked.shape
    inner = 128
    shaped = stacked.reshape(count, columns // LOOK_RNG, LOOK_RNG, pulse_len // inner, inner)
    summed = jnp.sum(shaped, axis=2)
    lanes = jnp.arange(inner, dtype=jnp.int32)
    groups = jnp.arange(inner // LOOK_AZ, dtype=jnp.int32)
    pool = (lanes[:, None] // LOOK_AZ == groups[None, :]).astype(jnp.float32)
    looked = jnp.einsum("nrab,bg->nrag", summed, pool, precision=lax.Precision.HIGHEST)
    scale = 1.0 / (LOOK_RNG * LOOK_AZ)
    return looked.reshape(count, columns // LOOK_RNG, pulse_len // LOOK_AZ) * scale


def cross_looks(own_block, partners):
    own_f = own_block.astype(jnp.float32)
    prods = []
    for partner in partners:
        other_f = partner.astype(jnp.float32)
        prods.append(own_f[0] * other_f[0] + own_f[1] * other_f[1])
        prods.append(own_f[1] * other_f[0] - own_f[0] * other_f[1])
    looked = multilook(jnp.stack(prods))
    return looked.reshape(len(partners), 2, *looked.shape[1:])


def per_device(raw_echo, chirp_phase, pulse_counts, azimuth_rate, partner_bits):
    echoes = raw_echo[0]
    pulses_dev = echoes.shape[1]
    block_cols = min(256, RNG)
    window = block_cols + TAPS - 1
    amplitude = 2.0 / math.sqrt(TAPS)
    table_re = (amplitude * jnp.cos(chirp_phase)).astype(jnp.bfloat16)
    table_im = (amplitude * jnp.sin(chirp_phase)).astype(jnp.bfloat16)
    padding = jnp.zeros((block_cols,), jnp.bfloat16)
    band_re = jnp.tile(jnp.concatenate([table_re, padding]), block_cols)[
        : block_cols * window
    ].reshape(block_cols, window)
    band_im = jnp.tile(jnp.concatenate([table_im, padding]), block_cols)[
        : block_cols * window
    ].reshape(block_cols, window)
    toeplitz = jnp.concatenate(
        [jnp.concatenate([band_re, band_im], axis=1), jnp.concatenate([-band_im, band_re], axis=1)],
        axis=0,
    )
    live_pulses = pulse_counts[0]
    first_pulse = lax.axis_index("pulse") * pulses_dev
    compressed = compress(echoes, toeplitz, first_pulse, live_pulses, block_cols, window)
    turned = lax.all_to_all(compressed, "pulse", split_axis=1, concat_axis=2, tiled=True)
    focused = azimuth(turned, azimuth_rate).astype(jnp.bfloat16)
    chosen = partner_bits[0]
    acq_size = lax.axis_size("acq")
    me = lax.axis_index("acq")
    me_parity = jnp.int32(0)
    for which in range(acq_size.bit_length() - 1):
        me_parity = me_parity ^ me >> which & 1
    low_bits = (0, 1)
    high_bits = (2, 3)
    edge_pairs = []
    for slot in range(2):
        edge_pairs.append(
            [
                (i, i ^ 1 << (high_bits[slot] if parity(i) else low_bits[slot]))
                for i in range(acq_size)
            ]
        )
    arrived = [lax.ppermute(focused, "acq", pairs) for pairs in edge_pairs]
    looked = cross_looks(focused, arrived)
    returned = [
        lax.ppermute(looked[slot], "acq", [(dst, src) for src, dst in edge_pairs[slot]])
        for slot in range(2)
    ]
    candidates = []
    for slot in range(2):
        recv_bit = jnp.where(me_parity == 1, low_bits[slot], high_bits[slot])
        send_bit = jnp.where(me_parity == 1, high_bits[slot], low_bits[slot])
        candidates.append((recv_bit, looked[slot]))
        back = returned[slot]
        candidates.append((send_bit, jnp.stack([back[0], -back[1]])))
    results = []
    for slot in range(2):
        pick = candidates[0][1]
        for bit, value in candidates[1:]:
            pick = jnp.where(chosen[slot] == bit, value, pick)
        results.append(pick)
    interfere_real = jnp.stack([item[0] for item in results])[None]
    interfere_imag = jnp.stack([item[1] for item in results])[None]
    return (interfere_real, interfere_imag)


def solution(mesh):
    in_specs = (P("acq", None, "pulse", None), P(), P("acq"), P("pulse"), P("acq", None))
    out_specs = (P("acq", None, "pulse", None), P("acq", None, "pulse", None))
    return jax.shard_map(
        per_device, mesh=mesh, in_specs=in_specs, out_specs=out_specs, check_vma=False
    )
```

profile of v0, /device:TPU:36, one launch (start us, length us, event | category | flops | bytes accessed | tf_op | source)
XLA Modules:
  0.0 113.7 jit_solution(9805634354367197942)
XLA Ops:
  0.6 0.7 multiply_convert_fusion
  1.4 0.8 tile.21
  2.2 1.2 %reshape.341 = bf16[256,1279]{1,0:T(8,128)(2,1)S(1)} reshape(bf16[327424]{0:T(1024)(128)(2,1)S(1)} %bitcast.138) | data formatting | bytes 1309696 | tf_op jit(solution)/shard_map/reshape | solution.py:137
  3.4 1.0 neg.61
  4.4 3.6 %copy.30 = bf16[1,2,256,1535]{3,2,1,0:T(8,128)(2,1)S(1)} copy(bf16[1,2,256,1535]{2,1,3,0:T(2,128)(2,1)} %param.5) | data formatting | bytes 3143680 | tf_op args[0]
  8.0 1.2 %slice_bitcast_fusion.3 = (bf16[256,1279]{1,0:T(8,128)(2,1)}, bf16[256,1279]{1,0:T(8,128)(2,1)S(1)}, bf16[256,1279]{1,0:T(8,128)(2,1)S(1)}, bf16[256,1279]{1,0:T(8,128)(2,1)}) fusion(bf16[2,256,1535]{2,1,0:T(8,128)(2,1)S(1)} %bitcast.137), kind=kLoop, calls=%fused_computation.38 | loop fusion | bytes 5238784 | tf_op jit(solution)/shard_map/squeeze | solution.py:33
  9.3 0.8 tile.9
  10.1 2.1 %reshape.340 = bf16[256,1279]{1,0:T(8,128)(2,1)} reshape(bf16[327424]{0:T(1024)(128)(2,1)S(1)} %bitcast.139) | data formatting | bytes 1309696 | tf_op jit(solution)/shard_map/reshape | solution.py:134
  12.1 3.0 %fusion.2 = f32[512,256]{1,0:T(8,128)S(1)} fusion(bf16[256,1279]{1,0:T(8,128)(2,1)} %get-tuple-element.9, bf16[256,1279]{1,0:T(8,128)(2,1)} %get-tuple-element.6, bf16[256,1279]{1,0:T(8,128)(2,1)} %reshape.340, bf16[256,1279]{1,0:T(8,128)(2,1)} %neg.61, bf16[256,1279]{1,0:T(8,128)(2,1)S(1)} %reshape.341), kind=kOutput, calls=%fused_computation.9 | convolution fusion | flops 683661312 | bytes 3798528 | tf_op jit(solution)/shard_map/dot_general | solution.py:34
  15.2 1.0 fusion.6
  17.1 1.4 %copy.31 = bf16[2,512,256]{2,0,1:T(2,128)(2,1)} copy(bf16[2,512,256]{2,1,0:T(8,128)(2,1)S(1)} %fusion.12) | data formatting | bytes 1048576 | tf_op jit(solution)/shard_map/convert_element_type | solution.py:42
  18.5 18.0 %all-to-all-start = ((bf16[2,512,256]{2,0,1:T(2,128)(2,1)}), bf16[2,512,256]{2,0,1:T(2,128)(2,1)S(1)}, u32[]{:S(2)}, u32[]{:S(2)}) async-start(bf16[2,512,256]{2,0,1:T(2,128)(2,1)} %copy.31), calls=%async_computation | async-start | bytes 1048576 | tf_op jit(solution)/shard_map/all_to_all | solution.py:145
  37.1 0.3 fusion.65
  37.3 0.3 fusion.59
  37.7 32.5 %all-to-all-done = bf16[2,512,256]{2,0,1:T(2,128)(2,1)S(1)} async-done(((bf16[2,512,256]{2,0,1:T(2,128)(2,1)}), bf16[2,512,256]{2,0,1:T(2,128)(2,1)S(1)}, u32[]{:S(2)}, u32[]{:S(2)}) %all-to-all-start) | async-done | bytes 524320 | tf_op jit(solution)/shard_map/all_to_all | solution.py:145
  70.2 0.3 copy.74
  70.7 0.6 convolution_bitcast_fusion.3
  71.5 1.0 convolution_bitcast_fusion.2
  72.5 2.1 %fusion.23 = (f32[1,16,64,128]{3,2,1,0:T(8,128)S(1)}, f32[1,16,64,128]{3,2,1,0:T(8,128)S(1)}) fusion(f32[2,16,64,128]{3,2,1,0:T(8,128)S(1)} %convolution_bitcast_fusion.2, f32[64,128]{1,0:T(8,128)S(1)} %fusion.56, f32[16]{0:T(128)S(1)} %broadcast_multiply_fusion), kind=kLoop, calls=%fused_computation.39 | loop fusion | flops 1048576 | bytes 2129984 | tf_op jit(solution)/shard_map/sub | solution.py:24
  74.6 1.0 convolution_bitcast_fusion.1
  75.8 1.1 fusion.11
  77.1 2.4 %collective-permute-start = (bf16[2,16,8192]{2,1,0:T(8,128)(2,1)S(1)}, bf16[2,16,8192]{2,1,0:T(8,128)(2,1)S(1)}, u32[]{:S(2)}, u32[]{:S(2)}) collective-permute-start(bf16[2,16,8192]{2,1,0:T(8,128)(2,1)S(1)} %convert_element_type.148), channel_id=1, source_target_pairs={{0,32},{32,160},{64,192},{96,64},{128,0},{160,128},{192,224},{224,... | collective-permute-start | bytes 1572872 | tf_op jit(solution)/shard_map/ppermute | solution.py:163
  79.6 2.1 %collective-permute-start.1 = (bf16[2,16,8192]{2,1,0:T(8,128)(2,1)S(1)}, bf16[2,16,8192]{2,1,0:T(8,128)(2,1)S(1)}, u32[]{:S(2)}, u32[]{:S(2)}) collective-permute-start(bf16[2,16,8192]{2,1,0:T(8,128)(2,1)S(1)} %convert_element_type.148), channel_id=1, source_target_pairs={{0,64},{32,288},{64,320},{96,32},{128,384},{160,224},{192,128},{22... | collective-permute-start | bytes 1572872 | tf_op jit(solution)/shard_map/ppermute | solution.py:163
  81.7 8.8 %collective-permute-done = bf16[2,16,8192]{2,1,0:T(8,128)(2,1)S(1)} collective-permute-done((bf16[2,16,8192]{2,1,0:T(8,128)(2,1)S(1)}, bf16[2,16,8192]{2,1,0:T(8,128)(2,1)S(1)}, u32[]{:S(2)}, u32[]{:S(2)}) %collective-permute-start) | collective-permute-done | bytes 524320 | tf_op jit(solution)/shard_map/ppermute | solution.py:163
  90.7 0.6 collective-permute-done.1
  92.2 0.7 convolution_multiply_fusion
  93.3 7.2 %collective-permute-start.2 = (f32[2,4,512]{2,1,0:T(4,128)S(1)}, f32[2,4,512]{2,1,0:T(4,128)S(1)}, u32[]{:S(2)}, u32[]{:S(2)}) collective-permute-start(f32[2,4,512]{2,1,0:T(4,128)S(1)} %slice.158), channel_id=1, source_target_pairs={{64,0},{288,32},{320,64},{32,96},{384,128},{224,160},{128,192},{48... | collective-permute-start | bytes 49160 | tf_op jit(solution)/shard_map/ppermute | solution.py:166
  100.5 0.6 fusion.86
  105.3 1.9 %collective-permute-start.3 = (f32[2,4,512]{2,1,0:T(4,128)S(1)}, f32[2,4,512]{2,1,0:T(4,128)S(1)}, u32[]{:S(2)}, u32[]{:S(2)}) collective-permute-start(f32[2,4,512]{2,1,0:T(4,128)S(1)} %slice.162), channel_id=1, source_target_pairs={{32,0},{160,32},{192,64},{64,96},{0,128},{128,160},{224,192},{96,2... | collective-permute-start | bytes 49160 | tf_op jit(solution)/shard_map/ppermute | solution.py:166
  107.2 5.2 %collective-permute-done.3 = f32[2,4,512]{2,1,0:T(4,128)S(1)} collective-permute-done((f32[2,4,512]{2,1,0:T(4,128)S(1)}, f32[2,4,512]{2,1,0:T(4,128)S(1)}, u32[]{:S(2)}, u32[]{:S(2)}) %collective-permute-start.3) | collective-permute-done | bytes 16416 | tf_op jit(solution)/shard_map/ppermute | solution.py:166
  112.4 0.6 maximum_bitcast_fusion.9
  113.1 0.6 maximum_bitcast_fusion.8
  (51 shorter events, 3.4 us)
Async XLA Ops:
  12.1 3.0 %copy-start = (bf16[256,1279]{1,0:T(8,128)(2,1)S(1)}, bf16[256,1279]{1,0:T(8,128)(2,1)}, u32[]{:S(2)}) copy-start(bf16[256,1279]{1,0:T(8,128)(2,1)} %neg.61) | copy-start | bytes 1964548
  12.1 3.1 %copy-start.1 = (bf16[256,1279]{1,0:T(8,128)(2,1)S(1)}, bf16[256,1279]{1,0:T(8,128)(2,1)}, u32[]{:S(2)}) copy-start(bf16[256,1279]{1,0:T(8,128)(2,1)} %reshape.340) | copy-start | bytes 1964548
  17.1 20.6 %copy-start.3 = (f32[16]{0:T(128)S(1)}, f32[16]{0:T(128)}, u32[]{:S(2)}) copy-start(f32[16]{0:T(128)} %param.8) | copy-start | bytes 196
  18.5 51.7 %all-to-all-start = ((bf16[2,512,256]{2,0,1:T(2,128)(2,1)}), bf16[2,512,256]{2,0,1:T(2,128)(2,1)S(1)}, u32[]{:S(2)}, u32[]{:S(2)}) async-start(bf16[2,512,256]{2,0,1:T(2,128)(2,1)} %copy.31), calls=%async_computation | async-start | bytes 1048576 | tf_op jit(solution)/shard_map/all_to_all | solution.py:145
  77.1 13.5 %collective-permute-start = (bf16[2,16,8192]{2,1,0:T(8,128)(2,1)S(1)}, bf16[2,16,8192]{2,1,0:T(8,128)(2,1)S(1)}, u32[]{:S(2)}, u32[]{:S(2)}) collective-permute-start(bf16[2,16,8192]{2,1,0:T(8,128)(2,1)S(1)} %convert_element_type.148), channel_id=1, source_target_pairs={{0,32},{32,160},{64,192},{96,64},{128,0},{160,128},{192,224},{224,... | collective-permute-start | bytes 1572872 | tf_op jit(solution)/shard_map/ppermute | solution.py:163
  79.6 11.7 %collective-permute-start.1 = (bf16[2,16,8192]{2,1,0:T(8,128)(2,1)S(1)}, bf16[2,16,8192]{2,1,0:T(8,128)(2,1)S(1)}, u32[]{:S(2)}, u32[]{:S(2)}) collective-permute-start(bf16[2,16,8192]{2,1,0:T(8,128)(2,1)S(1)} %convert_element_type.148), channel_id=1, source_target_pairs={{0,64},{32,288},{64,320},{96,32},{128,384},{160,224},{192,128},{22... | collective-permute-start | bytes 1572872 | tf_op jit(solution)/shard_map/ppermute | solution.py:163
  92.0 8.5 %copy-start.2 = (s32[1,2]{1,0:T(1,128)S(1)}, s32[1,2]{1,0:T(1,128)}, u32[]{:S(2)}) copy-start(s32[1,2]{1,0:T(1,128)} %param.9) | copy-start | bytes 28
  93.3 13.9 %collective-permute-start.2 = (f32[2,4,512]{2,1,0:T(4,128)S(1)}, f32[2,4,512]{2,1,0:T(4,128)S(1)}, u32[]{:S(2)}, u32[]{:S(2)}) collective-permute-start(f32[2,4,512]{2,1,0:T(4,128)S(1)} %slice.158), channel_id=1, source_target_pairs={{64,0},{288,32},{320,64},{32,96},{384,128},{224,160},{128,192},{48... | collective-permute-start | bytes 49160 | tf_op jit(solution)/shard_map/ppermute | solution.py:166
  105.3 7.1 %collective-permute-start.3 = (f32[2,4,512]{2,1,0:T(4,128)S(1)}, f32[2,4,512]{2,1,0:T(4,128)S(1)}, u32[]{:S(2)}, u32[]{:S(2)}) collective-permute-start(f32[2,4,512]{2,1,0:T(4,128)S(1)} %slice.162), channel_id=1, source_target_pairs={{32,0},{160,32},{192,64},{64,96},{0,128},{128,160},{224,192},{96,2... | collective-permute-start | bytes 49160 | tf_op jit(solution)/shard_map/ppermute | solution.py:166
where the time goes:
time: 114 us
  waiting for transfers between devices  47.1 us (41%)
  starting transfers between devices  31.6 us (28%)
  local copies, waits for them, and re-layouts  13.5 us (12%)
  matrix products  8.41 us (7%)
  other arithmetic  7.39 us (6%)
  between operations  5.63 us (5%)
    all_to_all x1, waiting for transfers between devices, per_device(): lax.all_to_all(compressed, 'pulse', split_axis=1, concat_axis=2, tiled=True)  32.5 us
    all_to_all x1, starting transfers between devices, per_device(): lax.all_to_all(compressed, 'pulse', split_axis=1, concat_axis=2, tiled=True)  18 us
    ppermute x2, waiting for transfers between devices, per_device(): arrived = [lax.ppermute(focused, 'acq', pairs) for pairs in edge_pairs]  9.46 us
    ppermute x2, starting transfers between devices, per_device(): lax.ppermute(looked[slot], 'acq', [(dst, src) for src, dst in edge_pairs[...  9.13 us
    ppermute x2, waiting for transfers between devices, per_device(): lax.ppermute(looked[slot], 'acq', [(dst, src) for src, dst in edge_pairs[...  5.19 us
    ppermute x2, starting transfers between devices, per_device(): arrived = [lax.ppermute(focused, 'acq', pairs) for pairs in edge_pairs]  4.51 us
    unnamed x13, local copies, waits for them, and re-layouts  4.04 us
    dot_general x2, matrix products, compress(): lax.dot_general(toeplitz, stacked, (((1,), (1,)), ((), ())), preferred_el...  3.99 us
  transfers between devices with their start and end apart: 5, of which 4 were waited for; matrix products, arithmetic and copies ran while one was open for 2% of the time, Pallas kernels for 0%

commit v1 on v0

--- a/solution.py
+++ b/solution.py
@@ -142,7 +142,10 @@
     live_pulses = pulse_counts[0]
     first_pulse = lax.axis_index("pulse") * pulses_dev
     compressed = compress(echoes, toeplitz, first_pulse, live_pulses, block_cols, window)
-    turned = lax.all_to_all(compressed, "pulse", split_axis=1, concat_axis=2, tiled=True)
+    peers = lax.axis_size("pulse")
+    shards = jnp.stack(jnp.split(compressed, peers, axis=1), axis=0)
+    shards = lax.all_to_all(shards, "pulse", split_axis=0, concat_axis=0)
+    turned = jnp.concatenate(shards, axis=2)
     focused = azimuth(turned, azimuth_rate).astype(jnp.bfloat16)
     chosen = partner_bits[0]
     acq_size = lax.axis_size("acq")

time: 114 us -> 132 us (1.16)
  local copies, waits for them, and re-layouts: 13.5 us -> 31.3 us
    unnamed x13 -> x44, local copies, waits for them, and re-layouts: 4.04 us -> 22.6 us
    convert_element_type x1 -> x0, local copies, waits for them, and re-layouts: 1.35 us -> none  [compress(): return (joined * keep[None, None, :]).astype(jnp.bfloat16)]
where the time goes in v1:
time: 132 us; the launch traced here: 131 us
  waiting for transfers between devices  47.1 us (36%)
  starting transfers between devices  31.6 us (24%)
  local copies, waits for them, and re-layouts  31.3 us (24%)
  matrix products  8.43 us (6%)
  other arithmetic  7.39 us (6%)
  between operations  5.64 us (4%)
    all_to_all x1, waiting for transfers between devices, per_device(): shards = lax.all_to_all(shards, 'pulse', split_axis=0, concat_axis=0)  32.5 us
    unnamed x44, local copies, waits for them, and re-layouts  22.6 us
    all_to_all x1, starting transfers between devices, per_device(): shards = lax.all_to_all(shards, 'pulse', split_axis=0, concat_axis=0)  18 us
    ppermute x2, waiting for transfers between devices, per_device(): arrived = [lax.ppermute(focused, 'acq', pairs) for pairs in edge_pairs]  9.45 us
    ppermute x2, starting transfers between devices, per_device(): lax.ppermute(looked[slot], 'acq', [(dst, src) for src, dst in edge_pairs[...  9.11 us
    ppermute x2, waiting for transfers between devices, per_device(): lax.ppermute(looked[slot], 'acq', [(dst, src) for src, dst in edge_pairs[...  5.19 us
    ppermute x2, starting transfers between devices, per_device(): arrived = [lax.ppermute(focused, 'acq', pairs) for pairs in edge_pairs]  4.5 us
    dot_general x2, matrix products, compress(): lax.dot_general(toeplitz, stacked, (((1,), (1,)), ((), ())), preferred_el...  3.99 us
  transfers between devices with their start and end apart: 5, of which 4 were waited for; matrix products, arithmetic and copies ran while one was open for 2% of the time, Pallas kernels for 0%

profile of v1, /device:TPU:36, one launch (start us, length us, event | category | flops | bytes accessed | tf_op | source)
XLA Modules:
  0.0 131.5 jit_solution(7584870578271528940)
XLA Ops:
  0.6 0.7 multiply_convert_fusion
  1.4 0.8 tile.21
  2.2 1.2 reshape.345
  3.4 1.0 neg.61
  4.4 3.6 %copy.18 = bf16[1,2,256,1535]{3,2,1,0:T(8,128)(2,1)S(1)} copy(bf16[1,2,256,1535]{2,1,3,0:T(2,128)(2,1)} %param.5) | data formatting | bytes 3143680 | tf_op args[0]
  8.0 1.2 slice_bitcast_fusion.3
  9.3 0.8 tile.9
  10.1 2.1 %reshape.344 = bf16[256,1279]{1,0:T(8,128)(2,1)} reshape(bf16[327424]{0:T(1024)(128)(2,1)S(1)} %bitcast.264) | data formatting | bytes 1309696 | tf_op jit(solution)/shard_map/reshape | solution.py:134
  12.1 3.0 %fusion.2 = f32[512,256]{1,0:T(8,128)S(1)} fusion(bf16[256,1279]{1,0:T(8,128)(2,1)} %get-tuple-element.9, bf16[256,1279]{1,0:T(8,128)(2,1)} %get-tuple-element.6, bf16[256,1279]{1,0:T(8,128)(2,1)} %reshape.344, bf16[256,1279]{1,0:T(8,128)(2,1)} %neg.61, bf16[256,1279]{1,0:T(8,128)(2,1)S(1)} %reshape.345), kind=kOutput, calls=%fused_computation.9 | convolution fusion | flops 683661312 | bytes 3798528 | tf_op jit(solution)/shard_map/dot_general | solution.py:34
  15.2 1.0 fusion.6
  19.5 0.6 constant_dynamic-update-slice_fusion.27
  20.1 0.6 constant_dynamic-update-slice_fusion.26
  25.5 0.6 constant_dynamic-update-slice_fusion.17
  32.7 0.6 constant_dynamic-update-slice_fusion.5
  33.9 0.6 constant_dynamic-update-slice_fusion.3
  36.3 18.0 %all-to-all-start = ((bf16[32,2,16,256]{3,2,1,0:T(8,128)(2,1)}), bf16[32,2,16,256]{3,2,1,0:T(8,128)(2,1)S(1)}, u32[]{:S(2)}, u32[]{:S(2)}) async-start(bf16[32,2,16,256]{3,2,1,0:T(8,128)(2,1)} %constant_dynamic-update-slice_fusion), calls=%async_computation | async-start | bytes 1048576 | tf_op jit(solution)/shard_map/all_to_all | solution.py:147
  55.6 32.5 %all-to-all-done = bf16[32,2,16,256]{3,2,1,0:T(8,128)(2,1)S(1)} async-done(((bf16[32,2,16,256]{3,2,1,0:T(8,128)(2,1)}), bf16[32,2,16,256]{3,2,1,0:T(8,128)(2,1)S(1)}, u32[]{:S(2)}, u32[]{:S(2)}) %all-to-all-start) | async-done | bytes 524320 | tf_op jit(solution)/shard_map/all_to_all | solution.py:147
  88.5 0.6 convolution_bitcast_fusion.3
  89.3 1.0 convolution_bitcast_fusion.2
  90.3 2.1 %fusion.23 = (f32[1,16,64,128]{3,2,1,0:T(8,128)S(1)}, f32[1,16,64,128]{3,2,1,0:T(8,128)S(1)}) fusion(f32[2,16,64,128]{3,2,1,0:T(8,128)S(1)} %convolution_bitcast_fusion.2, f32[64,128]{1,0:T(8,128)S(1)} %fusion.56, f32[16]{0:T(128)S(1)} %broadcast_multiply_fusion), kind=kLoop, calls=%fused_computation.39 | loop fusion | flops 1048576 | bytes 2129984 | tf_op jit(solution)/shard_map/sub | solution.py:24
  92.5 1.0 convolution_bitcast_fusion.1
  93.7 1.1 fusion.11
  95.0 2.4 %collective-permute-start = (bf16[2,16,8192]{2,1,0:T(8,128)(2,1)S(1)}, bf16[2,16,8192]{2,1,0:T(8,128)(2,1)S(1)}, u32[]{:S(2)}, u32[]{:S(2)}) collective-permute-start(bf16[2,16,8192]{2,1,0:T(8,128)(2,1)S(1)} %convert_element_type.148), channel_id=1, source_target_pairs={{0,32},{32,160},{64,192},{96,64},{128,0},{160,128},{192,224},{224,... | collective-permute-start | bytes 1572872 | tf_op jit(solution)/shard_map/ppermute | solution.py:166
  97.4 2.1 %collective-permute-start.1 = (bf16[2,16,8192]{2,1,0:T(8,128)(2,1)S(1)}, bf16[2,16,8192]{2,1,0:T(8,128)(2,1)S(1)}, u32[]{:S(2)}, u32[]{:S(2)}) collective-permute-start(bf16[2,16,8192]{2,1,0:T(8,128)(2,1)S(1)} %convert_element_type.148), channel_id=1, source_target_pairs={{0,64},{32,288},{64,320},{96,32},{128,384},{160,224},{192,128},{22... | collective-permute-start | bytes 1572872 | tf_op jit(solution)/shard_map/ppermute | solution.py:166
  99.6 8.8 %collective-permute-done = bf16[2,16,8192]{2,1,0:T(8,128)(2,1)S(1)} collective-permute-done((bf16[2,16,8192]{2,1,0:T(8,128)(2,1)S(1)}, bf16[2,16,8192]{2,1,0:T(8,128)(2,1)S(1)}, u32[]{:S(2)}, u32[]{:S(2)}) %collective-permute-start) | collective-permute-done | bytes 524320 | tf_op jit(solution)/shard_map/ppermute | solution.py:166
  108.4 0.7 collective-permute-done.1
  110.1 0.7 convolution_multiply_fusion
  111.1 7.2 %collective-permute-start.2 = (f32[2,4,512]{2,1,0:T(4,128)S(1)}, f32[2,4,512]{2,1,0:T(4,128)S(1)}, u32[]{:S(2)}, u32[]{:S(2)}) collective-permute-start(f32[2,4,512]{2,1,0:T(4,128)S(1)} %slice.158), channel_id=1, source_target_pairs={{64,0},{288,32},{320,64},{32,96},{384,128},{224,160},{128,192},{48... | collective-permute-start | bytes 49160 | tf_op jit(solution)/shard_map/ppermute | solution.py:169
  123.1 1.9 %collective-permute-start.3 = (f32[2,4,512]{2,1,0:T(4,128)S(1)}, f32[2,4,512]{2,1,0:T(4,128)S(1)}, u32[]{:S(2)}, u32[]{:S(2)}) collective-permute-start(f32[2,4,512]{2,1,0:T(4,128)S(1)} %slice.162), channel_id=1, source_target_pairs={{32,0},{160,32},{192,64},{64,96},{0,128},{128,160},{224,192},{96,2... | collective-permute-start | bytes 49160 | tf_op jit(solution)/shard_map/ppermute | solution.py:169
  125.0 5.2 %collective-permute-done.3 = f32[2,4,512]{2,1,0:T(4,128)S(1)} collective-permute-done((f32[2,4,512]{2,1,0:T(4,128)S(1)}, f32[2,4,512]{2,1,0:T(4,128)S(1)}, u32[]{:S(2)}, u32[]{:S(2)}) %collective-permute-start.3) | collective-permute-done | bytes 16416 | tf_op jit(solution)/shard_map/ppermute | solution.py:169
  130.3 0.6 maximum_bitcast_fusion.9
  130.9 0.6 maximum_bitcast_fusion.8
  (82 shorter events, 21.0 us)
Async XLA Ops:
  12.1 3.0 %copy-start = (bf16[256,1279]{1,0:T(8,128)(2,1)S(1)}, bf16[256,1279]{1,0:T(8,128)(2,1)}, u32[]{:S(2)}) copy-start(bf16[256,1279]{1,0:T(8,128)(2,1)} %neg.61) | copy-start | bytes 1964548
  12.1 3.1 %copy-start.1 = (bf16[256,1279]{1,0:T(8,128)(2,1)S(1)}, bf16[256,1279]{1,0:T(8,128)(2,1)}, u32[]{:S(2)}) copy-start(bf16[256,1279]{1,0:T(8,128)(2,1)} %reshape.344) | copy-start | bytes 1964548
  24.9 30.6 %copy-start.3 = (f32[16]{0:T(128)S(1)}, f32[16]{0:T(128)}, u32[]{:S(2)}) copy-start(f32[16]{0:T(128)} %param.8) | copy-start | bytes 196
  36.3 51.7 %all-to-all-start = ((bf16[32,2,16,256]{3,2,1,0:T(8,128)(2,1)}), bf16[32,2,16,256]{3,2,1,0:T(8,128)(2,1)S(1)}, u32[]{:S(2)}, u32[]{:S(2)}) async-start(bf16[32,2,16,256]{3,2,1,0:T(8,128)(2,1)} %constant_dynamic-update-slice_fusion), calls=%async_computation | async-start | bytes 1048576 | tf_op jit(solution)/shard_map/all_to_all | solution.py:147
  95.0 13.4 %collective-permute-start = (bf16[2,16,8192]{2,1,0:T(8,128)(2,1)S(1)}, bf16[2,16,8192]{2,1,0:T(8,128)(2,1)S(1)}, u32[]{:S(2)}, u32[]{:S(2)}) collective-permute-start(bf16[2,16,8192]{2,1,0:T(8,128)(2,1)S(1)} %convert_element_type.148), channel_id=1, source_target_pairs={{0,32},{32,160},{64,192},{96,64},{128,0},{160,128},{192,224},{224,... | collective-permute-start | bytes 1572872 | tf_op jit(solution)/shard_map/ppermute | solution.py:166
  97.4 11.7 %collective-permute-start.1 = (bf16[2,16,8192]{2,1,0:T(8,128)(2,1)S(1)}, bf16[2,16,8192]{2,1,0:T(8,128)(2,1)S(1)}, u32[]{:S(2)}, u32[]{:S(2)}) collective-permute-start(bf16[2,16,8192]{2,1,0:T(8,128)(2,1)S(1)} %convert_element_type.148), channel_id=1, source_target_pairs={{0,64},{32,288},{64,320},{96,32},{128,384},{160,224},{192,128},{22... | collective-permute-start | bytes 1572872 | tf_op jit(solution)/shard_map/ppermute | solution.py:166
  109.9 8.4 %copy-start.2 = (s32[1,2]{1,0:T(1,128)S(1)}, s32[1,2]{1,0:T(1,128)}, u32[]{:S(2)}) copy-start(s32[1,2]{1,0:T(1,128)} %param.9) | copy-start | bytes 28
  111.1 13.9 %collective-permute-start.2 = (f32[2,4,512]{2,1,0:T(4,128)S(1)}, f32[2,4,512]{2,1,0:T(4,128)S(1)}, u32[]{:S(2)}, u32[]{:S(2)}) collective-permute-start(f32[2,4,512]{2,1,0:T(4,128)S(1)} %slice.158), channel_id=1, source_target_pairs={{64,0},{288,32},{320,64},{32,96},{384,128},{224,160},{128,192},{48... | collective-permute-start | bytes 49160 | tf_op jit(solution)/shard_map/ppermute | solution.py:169
  123.1 7.1 %collective-permute-start.3 = (f32[2,4,512]{2,1,0:T(4,128)S(1)}, f32[2,4,512]{2,1,0:T(4,128)S(1)}, u32[]{:S(2)}, u32[]{:S(2)}) collective-permute-start(f32[2,4,512]{2,1,0:T(4,128)S(1)} %slice.162), channel_id=1, source_target_pairs={{32,0},{160,32},{192,64},{64,96},{0,128},{128,160},{224,192},{96,2... | collective-permute-start | bytes 49160 | tf_op jit(solution)/shard_map/ppermute | solution.py:169
